TPU v7x, 256 devices: a whole 4x4x8 slice. The times are simulated.
256 devices in a mesh: pair: 128 (over x, z, y), aux: 2 (over core).
Axes of the slice: x: 4, y: 4, z: 8, core: 2. Of those that a mesh axis runs over, the one named last changes fastest.
Arguments:
- amplitudes: bfloat16 [16384, 128, 128], P('pair', 'aux'), may hold values from -6 to 6
- k_term: bfloat16 [16384, 128, 128], P('pair', 'aux'), may hold values from -6 to 6
- margin_table: bfloat16 [1024, 128, 128], P('pair'), may hold values from -0.5 to 0.5
- margin_index: int32 [16384], P('pair'), may hold values from 0 to 7
- factors: bfloat16 [128, 512, 128], P('pair', 'aux'), may hold values from -6 to 6
- vir_energy: float32 [16384, 128], P('pair'), may hold values from 0.5 to 3
- occ_energy: float32 [128], replicated, may hold values from -2 to -0.3
- pair_owner: int32 [16384, 1], P('pair'), may hold values from 0 to 127; in each aligned block of 128 rows (0 to 127, 128 to 255, ...) at most 2 rows name the same one
Outputs:
- updated: bfloat16 [16384, 128, 128], P('pair', 'aux')
Inputs may be any that keep to these rules, and one draw needn't show every extreme that they name: `pair_owner`: no more than 2 of the 128 pairs of one aligned block name the same owner. `margin_index`: an index into the 8 margin blocks that belong to the pair's aligned block of 128 pairs.
All inputs are finite; a program needn't handle non-finite values.
Results may differ from a plain program's by a relative error of at most 0.0055.
Values may be sent and summed in bfloat16 or wider, within the bound.
No kernel may reach another device: no remote copies, remote signals or barrier semaphores. Data moves between devices by JAX's collectives and lax.ppermute only.
A program may use at most 128 MiB of HBM per device.

v0:
```python
import jax
import jax.numpy as jnp
from jax import lax
from jax.sharding import PartitionSpec as P


def local(
    amplitudes, k_term, margin_table, margin_index, factors, vir_energy, occ_energy, pair_owner
):
    axis_pairs = lax.axis_size("pair")
    aux_count = lax.axis_size("aux")
    own_index = lax.axis_index("pair")
    aux_index = lax.axis_index("aux")
    pair_count = amplitudes.shape[0]
    row_count = amplitudes.shape[1]
    vir_width = amplitudes.shape[2]
    aux_rows = factors.shape[1]
    ovl_count = margin_table.shape[0]
    capacity = max(2, (2 * pair_count + axis_pairs - 1) // axis_pairs)
    cycle_scale = float(vir_width * aux_rows * aux_count * pair_count) ** (-0.5)
    own_factors = factors[0]
    full_amp = lax.all_gather(amplitudes, "aux", axis=1, tiled=True)
    block_pick = (margin_index[:, None] == jnp.arange(ovl_count, dtype=jnp.int32)[None, :]).astype(
        jnp.bfloat16
    )
    margin = jnp.einsum(
        "po,oab->pab", block_pick, margin_table, preferred_element_type=jnp.float32
    ).astype(jnp.bfloat16)
    halfway = jnp.einsum(
        "pca,pab->pcb", full_amp, margin, preferred_element_type=jnp.float32
    ).astype(jnp.bfloat16)
    rotated = jnp.einsum(
        "pac,pab->pcb", margin, halfway, preferred_element_type=jnp.float32
    ).astype(jnp.bfloat16)
    partial_value = jnp.einsum(
        "pca,qa->pcq", rotated, own_factors, preferred_element_type=jnp.float32
    ).astype(jnp.bfloat16)
    pair_dest = pair_owner[:, 0]
    owner_hits = (pair_dest[:, None] == jnp.arange(axis_pairs, dtype=jnp.int32)[None, :]).astype(
        jnp.int32
    )
    slot_rank = jnp.sum(jnp.cumsum(owner_hits, axis=0) * owner_hits, axis=1) - 1
    slot_index = pair_dest * capacity + slot_rank
    outgoing = (
        jnp.zeros((axis_pairs * capacity, vir_width, aux_rows), jnp.bfloat16)
        .at[slot_index]
        .set(partial_value)
    )
    outgoing = outgoing.reshape(axis_pairs, capacity, vir_width, aux_rows)
    incoming = lax.all_to_all(outgoing, "pair", split_axis=0, concat_axis=0, tiled=True)
    slot_ones = jnp.ones((axis_pairs, capacity), jnp.bfloat16)
    summed = jnp.einsum(
        "sk,skcq->cq", slot_ones, incoming, preferred_element_type=jnp.float32
    ).astype(jnp.bfloat16)
    local_cycle = jnp.dot(summed, own_factors, preferred_element_type=jnp.float32)
    cycle_sum = lax.psum(local_cycle, "aux")
    cycle_vals = (cycle_scale * cycle_sum).astype(jnp.bfloat16)
    cycle_rows = cycle_vals.shape[0]
    slot_back = jnp.broadcast_to(
        cycle_vals[None, None], (axis_pairs, capacity, cycle_rows, vir_width)
    )
    returned = lax.all_to_all(slot_back, "pair", split_axis=0, concat_axis=0, tiled=True)
    own_cycle = returned.reshape(axis_pairs * capacity, cycle_rows, vir_width)[slot_index]
    own_cycle = lax.dynamic_slice_in_dim(own_cycle, aux_index * row_count, row_count, 1)
    cycle_term = jnp.einsum("pca,pba->pcb", own_cycle, margin, preferred_element_type=jnp.float32)
    occ_total = occ_energy.shape[0]
    occ_first = jnp.zeros((pair_count,), jnp.int32) + own_index
    both_ids = jnp.concatenate([occ_first, pair_dest])
    occ_select = (both_ids[:, None] == jnp.arange(occ_total, dtype=jnp.int32)[None, :]).astype(
        jnp.float32
    )
    occ_values = jnp.sum(occ_select * occ_energy[None, :], axis=1)
    occ_sum = occ_values[:pair_count] + occ_values[pair_count:]
    energy_rows = lax.dynamic_slice_in_dim(vir_energy, aux_index * row_count, row_count, 1)
    denominator = energy_rows[:, :, None] + vir_energy[:, None, :] - occ_sum[:, None, None]
    updated = (
        amplitudes.astype(jnp.float32) - (cycle_term + k_term.astype(jnp.float32)) / denominator
    )
    return updated.astype(jnp.bfloat16)


def solution(mesh):
    placed = (
        P("pair", "aux", None),
        P("pair", "aux", None),
        P("pair", None, None),
        P("pair"),
        P("pair", "aux", None),
        P("pair", None),
        P(),
        P("pair", None),
    )
    return jax.shard_map(
        local, mesh=mesh, in_specs=placed, out_specs=P("pair", "aux", None), check_vma=False
    )
```

profile of v0, /device:TPU:2, one launch (start us, length us, event | category | flops | bytes accessed | tf_op | source)
XLA Modules:
  0.0 725.3 jit_solution(5603408930430910391)
XLA Ops:
  6.5 0.0 copy-start
  6.5 0.0 all-gather.2.cloned.1.call-start
  6.5 0.7 all-gather.2.cloned.1.call-update
  7.3 0.0 all-reduce.3.cloned.1.call-start
  7.3 0.7 fusion.24
  8.1 0.2 reduce_window_sum.11
  8.2 0.8 select_reduce_fusion.1
  9.1 0.7 fusion.28
  9.7 0.0 copy-done
  9.7 3.9 convolution_convert_fusion.1
  13.6 17.5 %all-gather.2.cloned.1.call-done = bf16[128,128,128]{2,1,0:T(8,128)(2,1)} async-done(((bf16[128,64,128]{2,1,0:T(8,128)(2,1)}), bf16[128,128,128]{2,1,0:T(8,128)(2,1)}) %all-gather.2.cloned.1.call-update) | async-done | bytes 4194320 | tf_op jit(solution)/shard_map/all_gather | solution.py:22
  31.1 9.4 %fusion.11 = bf16[128,128,128]{2,1,0:T(8,128)(2,1)} fusion(bf16[128,128,128]{2,1,0:T(8,128)(2,1)} %all-gather.2.cloned.1.call-done, bf16[128,128,128]{2,0,1:T(8,128)(2,1)} %convolution_convert_fusion.1), kind=kOutput, calls=%fused_computation.10 | convolution fusion | flops 536870912 | bytes 12582912 | tf_op jit(solution)/shard_map/pca,pab->pcb/dot_general | solution.py:29
  40.5 0.0 copy-done.3
  40.5 11.1 %convolution_convert_fusion = bf16[128,128,256]{2,1,0:T(8,128)(2,1)} fusion(bf16[128,128,128]{2,1,0:T(8,128)(2,1)} %fusion.11, bf16[128,128,128]{2,0,1:T(8,128)(2,1)} %convolution_convert_fusion.1, bf16[1,256,128]{2,1,0:T(8,128)(2,1)S(1)} %copy-done.3), kind=kOutput, calls=%fused_computation.4 | convolution fusion | flops 1616904192 | bytes 16842752 | tf_op jit(solution)/shard_map/pca,qa->pcq/dot_general | solution.py:35
  51.6 6.0 broadcast_in_dim.7
  57.5 23.5 %scatter_fusion = bf16[256,128,256]{2,1,0:T(8,128)(2,1)} fusion(bf16[256,128,256]{2,1,0:T(8,128)(2,1)} %broadcast_in_dim.7, s32[128]{0:T(128)S(1)} %fusion.28, bf16[128,128,256]{2,1,0:T(8,128)(2,1)} %convolution_convert_fusion), kind=kCustom, calls=%fused_computation.1 | custom fusion | bytes 25166336 | tf_op jit(solution)/shard_map/scatter | solution.py:47
  81.0 381.3 %all_to_all.10 = bf16[128,2,128,256]{3,2,1,0:T(8,128)(2,1)S(1)} all-to-all(bf16[128,2,128,256]{3,2,1,0:T(8,128)(2,1)} %bitcast.23), channel_id=1, replica_groups=mesh['pair'=128,'aux'=2] {'pair'}, dimensions={0} | all-to-all | bytes 33554432 | tf_op jit(solution)/shard_map/all_to_all | solution.py:50
  462.3 8.9 %fusion = bf16[1,128,256,1]{2,0,3,1:T(2,128)(2,1)S(1)} fusion(bf16[128,2,128,256]{3,2,1,0:T(8,128)(2,1)S(1)} %all_to_all.10), kind=kOutput, calls=%fused_computation.2 | convolution fusion | flops 16777216 | bytes 16842752 | tf_op jit(solution)/shard_map/sk,skcq->cq/dot_general | solution.py:52
  471.2 0.8 fusion.21
  472.0 0.0 all-reduce.3.cloned.1.call-update
  472.0 23.3 %all-reduce.3.cloned.1.call-done = f32[128,128]{1,0:T(8,128)} async-done(((f32[128,128]{1,0:T(8,128)}), f32[128,128]{1,0:T(8,128)}) %all-reduce.3.cloned.1.call-update) | async-done | bytes 65552 | tf_op jit(solution)/shard_map/psum | solution.py:56
  495.3 0.8 multiply_convert_fusion
  496.1 5.3 broadcast_in_dim.8
  501.5 14.5 %all-to-all-start.1 = ((bf16[128,2,128,128]{3,2,1,0:T(8,128)(2,1)}), bf16[128,2,128,128]{3,2,1,0:T(8,128)(2,1)}, u32[]{:S(2)}, u32[]{:S(2)}) async-start(bf16[128,2,128,128]{3,2,1,0:T(8,128)(2,1)} %broadcast_in_dim.8), calls=%async_computation.1 | async-start | bytes 16777216 | tf_op jit(solution)/shard_map/all_to_all | solution.py:62
  516.0 0.0 copy-done.5
  516.0 0.0 copy-done.4
  516.0 0.1 constant_dynamic-slice_fusion
  516.1 0.0 copy-done.6
  516.1 0.2 select_reduce_fusion
  516.3 187.0 %all-to-all-done.1 = bf16[128,2,128,128]{3,2,1,0:T(8,128)(2,1)} async-done(((bf16[128,2,128,128]{3,2,1,0:T(8,128)(2,1)}), bf16[128,2,128,128]{3,2,1,0:T(8,128)(2,1)}, u32[]{:S(2)}, u32[]{:S(2)}) %all-to-all-start.1) | async-done | bytes 8388640 | tf_op jit(solution)/shard_map/all_to_all | solution.py:62
  703.3 6.6 gather_fusion
  709.8 8.6 %subtract_convert_fusion = bf16[128,64,128]{2,1,0:T(8,128)(2,1)} fusion(bf16[128,64,128]{2,1,0:T(8,128)(2,1)} %param.9, bf16[128,64,128]{2,1,0:T(8,128)(2,1)S(1)} %copy-done.2, f32[128]{0:T(128)S(1)} %slice_add_fusion, f32[128,128]{1,0:T(8,128)S(1)} %copy-done.4, f32[128,64]{1,0:T(8,128)S(1)} %constant_dynamic-slice_fusion, ...), kind=kOutput, calls=%fused_computation.5 | convolution fusion | flops 276824064 | bytes 12681732 | tf_op jit(solution)/shard_map/pca,pba->pcb/dot_general | solution.py:65
  (11 shorter events, 0.0 us)
Async XLA Ops:
  6.5 3.2 copy-start
  6.5 24.6 %all-gather.2.cloned.1.call-start = ((), (), s32[]{:S(2)}) async-start(), calls=%async_computation.2 | async-start | bytes 6291456 | tf_op jit(solution)/shard_map/all_gather | solution.py:22
  7.3 488.0 %all-reduce.3.cloned.1.call-start = ((), (), s32[]{:S(2)}) async-start(), calls=%async_computation.3 | async-start | bytes 131072 | tf_op jit(solution)/shard_map/psum | solution.py:56
  13.6 26.9 %copy-start.3 = (bf16[1,256,128]{2,1,0:T(8,128)(2,1)S(1)}, bf16[1,256,128]{2,1,0:T(8,128)(2,1)}, u32[]{:S(2)}) copy-start(bf16[1,256,128]{2,1,0:T(8,128)(2,1)} %param.12) | copy-start | bytes 196612
  501.5 14.5 %copy-start.5 = (s32[128,1]{0,1:T(1,128)S(1)}, s32[128,1]{0,1:T(1,128)}, u32[]{:S(2)}) copy-start(s32[128,1]{0,1:T(1,128)} %param.15) | copy-start | bytes 1540
  501.5 14.5 %copy-start.4 = (f32[128,128]{1,0:T(8,128)S(1)}, f32[128,128]{1,0:T(8,128)}, u32[]{:S(2)}) copy-start(f32[128,128]{1,0:T(8,128)} %param.13) | copy-start | bytes 196612
  501.5 14.6 %copy-start.6 = (f32[128]{0:T(128)S(1)}, f32[128]{0:T(128)}, u32[]{:S(2)}) copy-start(f32[128]{0:T(128)} %param.14) | copy-start | bytes 1540
  501.5 201.8 %all-to-all-start.1 = ((bf16[128,2,128,128]{3,2,1,0:T(8,128)(2,1)}), bf16[128,2,128,128]{3,2,1,0:T(8,128)(2,1)}, u32[]{:S(2)}, u32[]{:S(2)}) async-start(bf16[128,2,128,128]{3,2,1,0:T(8,128)(2,1)} %broadcast_in_dim.8), calls=%async_computation.1 | async-start | bytes 16777216 | tf_op jit(solution)/shard_map/all_to_all | solution.py:62
  703.3 6.6 copy-start.2
  709.8 8.6 %copy-start.1 = (bf16[8,128,128]{2,1,0:T(8,128)(2,1)S(1)}, bf16[8,128,128]{2,1,0:T(8,128)(2,1)}, u32[]{:S(2)}) copy-start(bf16[8,128,128]{2,1,0:T(8,128)(2,1)} %param.10) | copy-start | bytes 786436
Sparse Core Ops, SparseCore 0:
  9.1 21.9 all-gather.1
  472.1 23.1 all-reduce.2
where the time goes:
time: 726 us; the launch traced here: 725 us
  blocking collectives  381 us (52%)
  waiting for transfers between devices  229 us (32%)
  matrix products  42.6 us (6%)
  local copies, waits for them, and re-layouts  41.4 us (6%)
  starting transfers between devices  14.5 us (2%)
  between operations  13.5 us (2%)
    all_to_all x1, blocking collectives, local(): lax.all_to_all(outgoing, 'pair', split_axis=0, concat_axis=0, tiled=True)  381 us
    all_to_all x1, waiting for transfers between devices, local(): lax.all_to_all(slot_back, 'pair', split_axis=0, concat_axis=0, tiled=True)  187 us
    scatter x1, local copies, waits for them, and re-layouts, local(): outgoing = jnp.zeros((axis_pairs * capacity, vir_width, aux_rows), jnp.bf...  23.5 us
    psum x1, waiting for transfers between devices, local(): cycle_sum = lax.psum(local_cycle, 'aux')  23.3 us
    all_gather x1, waiting for transfers between devices, local(): full_amp = lax.all_gather(amplitudes, 'aux', axis=1, tiled=True)  17.5 us
  transfers between devices with their start and end apart: 3, of which 3 were waited for; matrix products, arithmetic and copies ran while one was open for 1% of the time, Pallas kernels for 0%

commit v1 on v0

--- a/solution.py
+++ b/solution.py
@@ -1,7 +1,15 @@
+import functools
 import jax
 import jax.numpy as jnp
 from jax import lax
 from jax.sharding import PartitionSpec as P
+
+
+def clusters_mark(t0, mesh_ax):
+    return jax.lax.all_gather(t0, axis_name=mesh_ax).sum(axis=0)
+
+
+pair_the_panels = functools.partial(clusters_mark, mesh_ax="aux")
 
 
 def local(
@@ -53,7 +61,7 @@
         "sk,skcq->cq", slot_ones, incoming, preferred_element_type=jnp.float32
     ).astype(jnp.bfloat16)
     local_cycle = jnp.dot(summed, own_factors, preferred_element_type=jnp.float32)
-    cycle_sum = lax.psum(local_cycle, "aux")
+    cycle_sum = pair_the_panels(local_cycle)
     cycle_vals = (cycle_scale * cycle_sum).astype(jnp.bfloat16)
     cycle_rows = cycle_vals.shape[0]
     slot_back = jnp.broadcast_to(

time: 726 us -> 697 us (0.960)
  waiting for transfers between devices: 229 us -> 205 us
    psum x1 -> x0, waiting for transfers between devices: 23.3 us -> none  [local(): cycle_sum = lax.psum(local_cycle, 'aux')]
  transfers between devices with their start and end apart: 3 -> 2, of which waited for: 3 -> 2; matrix products, arithmetic and copies ran while one was open for 1% -> 1% of each run, Pallas kernels for 0% -> 0%
where the time goes in v1:
time: 697 us; the launch traced here: 696 us
  blocking collectives  383 us (55%)
  waiting for transfers between devices  205 us (29%)
  matrix products  42 us (6%)
  local copies, waits for them, and re-layouts  41.3 us (6%)
  between operations  13.5 us (2%)
  starting transfers between devices  8.22 us (1%)
    all_to_all x1, blocking collectives, local(): lax.all_to_all(outgoing, 'pair', split_axis=0, concat_axis=0, tiled=True)  381 us
    all_to_all x1, waiting for transfers between devices, local(): lax.all_to_all(slot_back, 'pair', split_axis=0, concat_axis=0, tiled=True)  187 us
    scatter x1, local copies, waits for them, and re-layouts, local(): outgoing = jnp.zeros((axis_pairs * capacity, vir_width, aux_rows), jnp.bf...  23.3 us
    all_gather x1, waiting for transfers between devices, local(): full_amp = lax.all_gather(amplitudes, 'aux', axis=1, tiled=True)  17.5 us
  transfers between devices with their start and end apart: 2, of which 2 were waited for; matrix products, arithmetic and copies ran while one was open for 1% of the time, Pallas kernels for 0%

profile of v1, /device:TPU:2, one launch (start us, length us, event | category | flops | bytes accessed | tf_op | source)
XLA Modules:
  0.0 696.3 jit_solution(3616004471943296839)
XLA Ops:
  6.5 0.0 copy-start
  6.5 0.0 all-gather.3.cloned.1.call-start
  6.5 0.7 all-gather.3.cloned.1.call-update
  7.3 0.7 fusion.24
  8.0 0.2 reduce_window_sum.11
  8.2 0.8 select_reduce_fusion.1
  9.0 0.7 fusion.28
  9.7 0.0 copy-done
  9.7 3.9 convolution_convert_fusion.1
  13.6 0.0 copy-start.3
  13.6 17.5 %all-gather.3.cloned.1.call-done = bf16[128,128,128]{2,1,0:T(8,128)(2,1)} async-done(((bf16[128,64,128]{2,1,0:T(8,128)(2,1)}), bf16[128,128,128]{2,1,0:T(8,128)(2,1)}) %all-gather.3.cloned.1.call-update) | async-done | bytes 4194320 | tf_op jit(solution)/shard_map/all_gather | solution.py:30
  31.1 9.4 %fusion.11 = bf16[128,128,128]{2,1,0:T(8,128)(2,1)} fusion(bf16[128,128,128]{2,1,0:T(8,128)(2,1)} %all-gather.3.cloned.1.call-done, bf16[128,128,128]{2,0,1:T(8,128)(2,1)} %convolution_convert_fusion.1), kind=kOutput, calls=%fused_computation.10 | convolution fusion | flops 536870912 | bytes 12582912 | tf_op jit(solution)/shard_map/pca,pab->pcb/dot_general | solution.py:37
  40.5 0.0 copy-done.3
  40.5 11.1 %convolution_convert_fusion = bf16[128,128,256]{2,1,0:T(8,128)(2,1)} fusion(bf16[128,128,128]{2,1,0:T(8,128)(2,1)} %fusion.11, bf16[128,128,128]{2,0,1:T(8,128)(2,1)} %convolution_convert_fusion.1, bf16[1,256,128]{2,1,0:T(8,128)(2,1)S(1)} %copy-done.3), kind=kOutput, calls=%fused_computation.4 | convolution fusion | flops 1616904192 | bytes 16842752 | tf_op jit(solution)/shard_map/pca,qa->pcq/dot_general | solution.py:43
  51.6 6.0 broadcast_in_dim.7
  57.5 23.3 %scatter_fusion = bf16[256,128,256]{2,1,0:T(8,128)(2,1)} fusion(bf16[256,128,256]{2,1,0:T(8,128)(2,1)} %broadcast_in_dim.7, s32[128]{0:T(128)S(1)} %fusion.28, bf16[128,128,256]{2,1,0:T(8,128)(2,1)} %convolution_convert_fusion), kind=kCustom, calls=%fused_computation.1 | custom fusion | bytes 25166336 | tf_op jit(solution)/shard_map/scatter | solution.py:55
  80.9 381.4 %all_to_all.10 = bf16[128,2,128,256]{3,2,1,0:T(8,128)(2,1)S(1)} all-to-all(bf16[128,2,128,256]{3,2,1,0:T(8,128)(2,1)} %bitcast.24), channel_id=1, replica_groups=mesh['pair'=128,'aux'=2] {'pair'}, dimensions={0} | all-to-all | bytes 33554432 | tf_op jit(solution)/shard_map/all_to_all | solution.py:58
  462.3 8.9 %fusion = bf16[1,128,256,1]{2,0,3,1:T(2,128)(2,1)S(1)} fusion(bf16[128,2,128,256]{3,2,1,0:T(8,128)(2,1)S(1)} %all_to_all.10), kind=kOutput, calls=%fused_computation.2 | convolution fusion | flops 16777216 | bytes 16842752 | tf_op jit(solution)/shard_map/sk,skcq->cq/dot_general | solution.py:60
  471.2 0.1 fusion.21
  471.3 1.9 all-gather
  473.2 5.3 broadcast_in_dim.8
  478.6 8.2 %all-to-all-start.1 = ((bf16[128,2,128,128]{3,2,1,0:T(8,128)(2,1)}), bf16[128,2,128,128]{3,2,1,0:T(8,128)(2,1)}, u32[]{:S(2)}, u32[]{:S(2)}) async-start(bf16[128,2,128,128]{3,2,1,0:T(8,128)(2,1)} %broadcast_in_dim.8), calls=%async_computation.1 | async-start | bytes 16777216 | tf_op jit(solution)/shard_map/all_to_all | solution.py:70
  486.8 0.0 copy-done.5
  486.8 0.0 copy-done.4
  486.8 0.1 constant_dynamic-slice_fusion
  486.9 0.0 copy-done.6
  486.9 0.2 select_reduce_fusion
  487.1 187.1 %all-to-all-done.1 = bf16[128,2,128,128]{3,2,1,0:T(8,128)(2,1)} async-done(((bf16[128,2,128,128]{3,2,1,0:T(8,128)(2,1)}), bf16[128,2,128,128]{3,2,1,0:T(8,128)(2,1)}, u32[]{:S(2)}, u32[]{:S(2)}) %all-to-all-start.1) | async-done | bytes 8388640 | tf_op jit(solution)/shard_map/all_to_all | solution.py:70
  674.2 6.6 gather_fusion
  680.8 0.0 copy-done.2
  680.8 8.6 %subtract_convert_fusion = bf16[128,64,128]{2,1,0:T(8,128)(2,1)} fusion(bf16[128,64,128]{2,1,0:T(8,128)(2,1)} %param.9, bf16[128,64,128]{2,1,0:T(8,128)(2,1)S(1)} %copy-done.2, f32[128]{0:T(128)S(1)} %slice_add_fusion, f32[128,128]{1,0:T(8,128)S(1)} %copy-done.4, f32[128,64]{1,0:T(8,128)S(1)} %constant_dynamic-slice_fusion, ...), kind=kOutput, calls=%fused_computation.5 | convolution fusion | flops 276824064 | bytes 12681732 | tf_op jit(solution)/shard_map/pca,pba->pcb/dot_general | solution.py:73
  689.4 0.0 copy-done.1
  (10 shorter events, 0.0 us)
Async XLA Ops:
  6.5 3.1 copy-start
  6.5 24.6 %all-gather.3.cloned.1.call-start = ((), (), s32[]{:S(2)}) async-start(), calls=%async_computation.2 | async-start | bytes 6291456 | tf_op jit(solution)/shard_map/all_gather | solution.py:30
  13.6 26.9 %copy-start.3 = (bf16[1,256,128]{2,1,0:T(8,128)(2,1)S(1)}, bf16[1,256,128]{2,1,0:T(8,128)(2,1)}, u32[]{:S(2)}) copy-start(bf16[1,256,128]{2,1,0:T(8,128)(2,1)} %param.12) | copy-start | bytes 196612
  478.6 8.2 %copy-start.5 = (s32[128,1]{0,1:T(1,128)S(1)}, s32[128,1]{0,1:T(1,128)}, u32[]{:S(2)}) copy-start(s32[128,1]{0,1:T(1,128)} %param.15) | copy-start | bytes 1540
  478.6 8.3 %copy-start.4 = (f32[128,128]{1,0:T(8,128)S(1)}, f32[128,128]{1,0:T(8,128)}, u32[]{:S(2)}) copy-start(f32[128,128]{1,0:T(8,128)} %param.13) | copy-start | bytes 196612
  478.6 8.4 %copy-start.6 = (f32[128]{0:T(128)S(1)}, f32[128]{0:T(128)}, u32[]{:S(2)}) copy-start(f32[128]{0:T(128)} %param.14) | copy-start | bytes 1540
  478.6 195.6 %all-to-all-start.1 = ((bf16[128,2,128,128]{3,2,1,0:T(8,128)(2,1)}), bf16[128,2,128,128]{3,2,1,0:T(8,128)(2,1)}, u32[]{:S(2)}, u32[]{:S(2)}) async-start(bf16[128,2,128,128]{3,2,1,0:T(8,128)(2,1)} %broadcast_in_dim.8), calls=%async_computation.1 | async-start | bytes 16777216 | tf_op jit(solution)/shard_map/all_to_all | solution.py:70
  674.2 6.6 copy-start.2
  680.8 8.6 %copy-start.1 = (bf16[8,128,128]{2,1,0:T(8,128)(2,1)S(1)}, bf16[8,128,128]{2,1,0:T(8,128)(2,1)}, u32[]{:S(2)}) copy-start(bf16[8,128,128]{2,1,0:T(8,128)(2,1)} %param.10) | copy-start | bytes 786436
Sparse Core Ops, SparseCore 0:
  9.1 21.9 all-gather.2
